TPU v7x, 32 devices: a whole 2x2x4 slice. The times are simulated.
32 devices in a mesh: groups: 2 (over y), tm: 4 (over z), space: 2 (over x), dp: 2 (over core).
Axes of the slice: x: 2, y: 2, z: 4, core: 2. Of those that a mesh axis runs over, the one named last changes fastest.
Arguments:
- video_input: bfloat16 [4, 4, 8, 256, 96], P(('groups', 'dp'), 'tm', 'space'), parts along dimension 0, may hold values from -48 to 48
- out_cotangent: bfloat16 [4, 4, 8, 256, 96], P(('groups', 'dp'), 'tm', 'space'), parts along dimension 0, may hold values from -6 to 6
- conv_weight: bfloat16 [3, 3, 3, 96, 96], replicated, may hold values from -0.125 to 0.125
- sketch_signs: int32 [2, 96, 32], replicated, may hold values from 0 to 1
Outputs:
- input_grad: bfloat16 [4, 4, 8, 256, 96], P(('groups', 'dp'), 'tm', 'space'), parts along dimension 0
- weight_grad: float32 [6, 3, 3, 96, 96], P('groups'), parts along dimension 0
- sketches: float32 [4, 96, 32], P('groups'), parts along dimension 0
There are 2 independent parts, one for each index of `groups`. A program takes and returns all parts, laid end to end along the dimension named above; an argument that names none is the same for every part. Nothing has to cross between parts.
All inputs are finite; a program needn't handle non-finite values.
Results may differ from a plain program's by a relative error of at most 0.0025.
Values may be sent and summed in bfloat16 or wider, within the bound.
No kernel may reach another device: no remote copies, remote signals or barrier semaphores. Data moves between devices by JAX's collectives and lax.ppermute only.
A program may use at most 64 MiB of HBM per device.

v0:
```python
import jax
import jax.numpy as jnp
from jax import lax
from jax.sharding import PartitionSpec as P


def padded(value, sides, width):
    for axis, dim in sides:
        peers, length = (lax.axis_size(axis), value.shape[dim])
        up = [(i, (i + 1) % peers) for i in range(peers - 1)]
        down = [(j, i) for i, j in up]
        last = lax.slice_in_dim(value, length - width, length, axis=dim)
        leading = lax.slice_in_dim(value, 0, width, axis=dim)
        before = lax.ppermute(last, axis, up)
        after = lax.ppermute(leading, axis, down)
        value = jnp.concatenate([before, value, after], axis=dim)
    return value


def passed_along(block, axis, distance):
    devices = range(lax.axis_size(axis))
    route = [(i - distance, i) for i in devices if i - distance in devices]
    return lax.ppermute(block, axis, route)


def silu_slope(value):
    sig = jax.nn.sigmoid(value)
    return sig * (1.0 + value * (1.0 - sig))


def pad_columns(field):
    return jnp.pad(field, ((0, 0), (0, 0), (1, 1), (0, 0)))


def contract_rows(left, right):
    return lax.dot_general(
        left, right, (((0,), (0,)), ((), ())), preferred_element_type=jnp.float32
    )


def on_device(video_input, out_cotangent, conv_weight, sketch_signs):
    xin = video_input[:, 0]
    grad_out = out_cotangent[:, 0]
    batch, rows, width, chans = xin.shape
    count = batch * rows * width
    hidden = jax.nn.silu(xin.astype(jnp.float32)).astype(jnp.bfloat16)
    hid_flat = hidden.reshape(count, chans)
    grad_flat = grad_out.reshape(count, chans)
    grad_rows = padded(grad_out, (("space", 1),), 1)
    grad_frames = [pad_columns(grad_rows)]
    for lag in (1, 2):
        grad_frames.append(pad_columns(passed_along(grad_rows, "tm", -lag)))
    hid_rows = padded(hidden, (("space", 1),), 1)
    hid_frames = [pad_columns(hid_rows)]
    for lag in (1, 2):
        hid_frames.append(pad_columns(passed_along(hid_rows, "tm", lag)))
    grad_hidden = jnp.zeros((count, chans), jnp.float32)
    kernel_terms = []
    for a in range(3):
        for b in range(3):
            source = grad_frames[2 - a]
            slab = jnp.concatenate(
                [source[:, 2 - b : 2 - b + rows, 2 - e : 2 - e + width, :] for e in range(3)],
                axis=-1,
            ).reshape(count, 3 * chans)
            weight_mat = jnp.transpose(conv_weight[a, b], (0, 2, 1)).reshape(3 * chans, chans)
            grad_hidden = grad_hidden + jnp.dot(
                slab, weight_mat, preferred_element_type=jnp.float32
            )
            earlier = hid_frames[2 - a]
            hid_slab = jnp.concatenate(
                [earlier[:, b : b + rows, e : e + width, :] for e in range(3)], axis=-1
            ).reshape(count, 3 * chans)
            kernel_terms.append(contract_rows(hid_slab, grad_flat).reshape(3, chans, chans))
    kernel_local = jnp.stack(kernel_terms).reshape(3, 3, 3, chans, chans)
    xflat = xin.reshape(count, chans).astype(jnp.float32)
    input_grad = (grad_hidden * silu_slope(xflat)).astype(jnp.bfloat16)
    input_grad = input_grad.reshape(batch, 1, rows, width, chans)
    omega = (2 * sketch_signs - 1).astype(jnp.float32)
    cov_hidden = contract_rows(hid_flat, hid_flat)
    cov_grad = contract_rows(grad_flat, grad_flat)
    sketch_terms = jnp.stack(
        [
            jnp.dot(cov_hidden, omega[0], precision=lax.Precision.HIGHEST),
            jnp.dot(cov_grad, omega[1], precision=lax.Precision.HIGHEST),
        ]
    )
    total_pixels = (
        count
        * video_input.shape[1]
        * lax.axis_size("tm")
        * lax.axis_size("space")
        * lax.axis_size("dp")
    )
    sketch_total = lax.psum(sketch_terms, ("tm", "space", "dp"))
    kernel_total = lax.psum(kernel_local, ("tm", "space", "dp"))
    sketches = sketch_total / jnp.float32(total_pixels)
    weight_grad = kernel_total * (1.0 / jnp.sqrt(jnp.float32(total_pixels)))
    return (input_grad, weight_grad, sketches)


def solution(mesh):
    in_specs = (
        P(("groups", "dp"), "tm", "space", None, None),
        P(("groups", "dp"), "tm", "space", None, None),
        P(),
        P(),
    )
    out_specs = (
        P(("groups", "dp"), "tm", "space", None, None),
        P("groups", None, None, None, None),
        P("groups", None, None),
    )
    return jax.shard_map(
        on_device, mesh=mesh, in_specs=in_specs, out_specs=out_specs, check_vma=False
    )
```

profile of v0, /device:TPU:0, one launch (start us, length us, event | category | flops | bytes accessed | tf_op | source)
XLA Modules:
  0.0 231.1 jit_solution(7625184018858395198)
XLA Ops:
  7.2 0.9 fusion.34
  8.2 1.3 collective-permute-start.1
  9.4 4.9 %collective-permute-start = (bf16[1,1,256,96]{2,3,1,0:T(8,128)(2,1)S(1)}, bf16[1,1,256,96]{2,3,1,0:T(8,128)(2,1)S(1)}, u32[]{:S(2)}, u32[]{:S(2)}) collective-permute-start(bf16[1,1,256,96]{2,3,1,0:T(8,128)(2,1)S(1)} %get-tuple-element.72), channel_id=1, source_target_pairs={{0,2},{1,3},{4,6},{5,7},{8,10},{9,11},{12,14},{13,15},{16,18},{17,... | collective-permute-start | bytes 147464 | tf_op jit(solution)/shard_map/ppermute | solution.py:14
  14.3 1.0 fusion.27
  15.4 1.3 collective-permute-start.5
  16.7 4.5 %collective-permute-start.4 = (bf16[1,1,256,96]{2,3,1,0:T(8,128)(2,1)S(1)}, bf16[1,1,256,96]{2,3,1,0:T(8,128)(2,1)S(1)}, u32[]{:S(2)}, u32[]{:S(2)}) collective-permute-start(bf16[1,1,256,96]{2,3,1,0:T(8,128)(2,1)S(1)} %get-tuple-element.68), channel_id=1, source_target_pairs={{0,2},{1,3},{4,6},{5,7},{8,10},{9,11},{12,14},{13,15},{16,18},{17,... | collective-permute-start | bytes 147464 | tf_op jit(solution)/shard_map/ppermute | solution.py:14
  21.2 1.1 copy.31
  22.9 0.6 copy-done.5
  23.7 0.5 copy-done.18
  24.6 59.7 %psum.15 = f32[2,96,32]{1,2,0:T(8,128)S(1)} all-reduce(f32[2,96,32]{1,2,0:T(8,128)S(1)} %pad_maximum_fusion.19), channel_id=1, replica_groups=mesh['groups'=2,'tm'=4,'space'=2,'dp'=2] {'tm','space','dp'}, use_global_device_ids=true, to_apply=%region_1.2 | all-reduce | flops 6144 | bytes 49152 | tf_op jit(solution)/shard_map/psum | solution.py:95
  84.3 0.6 broadcast_multiply_fusion.1
  85.1 0.7 copy.43
  85.8 0.7 copy.44
  86.6 0.7 copy.45
  87.3 0.7 copy.46
  88.0 0.7 copy.47
  88.8 0.7 copy.48
  89.5 0.7 copy.49
  90.2 0.7 copy.50
  91.1 0.7 copy.60
  91.8 0.7 copy.51
  92.5 1.3 collective-permute-start.2
  93.8 1.3 collective-permute-start.3
  95.6 6.1 %collective-permute-start.6 = (bf16[1,6,256,96]{2,3,1,0:T(8,128)(2,1)S(1)}, bf16[1,6,256,96]{2,3,1,0:T(8,128)(2,1)S(1)}, u32[]{:S(2)}, u32[]{:S(2)}) collective-permute-start(bf16[1,6,256,96]{2,3,1,0:T(8,128)(2,1)S(1)} %pad_maximum_fusion.18), channel_id=1, source_target_pairs={{0,8},{4,12},{1,9},{5,13},{2,10},{6,14},{3,11},{7,15},{16,24},{20,... | collective-permute-start | bytes 884744 | tf_op jit(solution)/shard_map/ppermute | solution.py:23
  101.7 4.1 %collective-permute-start.7 = (bf16[1,6,256,96]{2,3,1,0:T(8,128)(2,1)S(1)}, bf16[1,6,256,96]{2,3,1,0:T(8,128)(2,1)S(1)}, u32[]{:S(2)}, u32[]{:S(2)}) collective-permute-start(bf16[1,6,256,96]{2,3,1,0:T(8,128)(2,1)S(1)} %pad_maximum_fusion.18), channel_id=1, source_target_pairs={{0,4},{4,8},{8,12},{1,5},{5,9},{9,13},{2,6},{6,10},{10,14},{3,7},{... | collective-permute-start | bytes 884744 | tf_op jit(solution)/shard_map/ppermute | solution.py:23
  106.9 0.5 copy.23
  107.7 0.7 copy.61
  108.5 0.7 copy.59
  109.7 0.9 copy.62
  111.2 0.5 copy.41
  113.4 0.5 copy.11
  114.0 0.5 copy.13
  114.6 0.5 copy.15
  115.1 0.5 copy.17
  115.7 0.5 copy.19
  116.2 0.9 copy.56
  117.6 0.9 copy.57
  118.6 0.5 copy.32
  119.1 0.5 copy.33
  119.8 0.5 copy.34
  120.4 0.5 pad_slice_fusion.7
  121.5 0.7 copy.36
  122.3 0.5 copy.37
  125.8 1.1 copy-done.3
  126.9 1.2 fusion.35
  132.4 0.7 copy.42
  133.1 88.6 %all-reduce.8.cloned.1.call-done = f32[3,3,3,96,96]{4,3,2,1,0:T(8,128)} async-done(((f32[3,3,3,96,96]{4,3,2,1,0:T(8,128)}), f32[3,3,3,96,96]{4,3,2,1,0:T(8,128)}) %all-reduce.8.cloned.1.call-update) | async-done | bytes 995344 | tf_op jit(solution)/shard_map/psum | solution.py:96
  221.7 2.5 %broadcast_multiply_fusion = f32[3,3,3,96,96]{4,3,2,1,0:T(8,128)} fusion(f32[3,3,3,96,96]{4,3,2,1,0:T(8,128)} %all-reduce.8.cloned.1.call-done), kind=kLoop, calls=%fused_computation.32 | loop fusion | flops 248832 | bytes 1990656 | tf_op jit(solution)/shard_map/mul | solution.py:98
  (116 shorter events, 15.2 us)
Async XLA Ops:
  7.2 15.2 %copy-start = (bf16[1,1,4,256,96]{3,4,2,1,0:T(8,128)(2,1)S(1)}, bf16[1,1,4,256,96]{3,4,2,1,0:T(8,128)(2,1)}, u32[]{:S(2)}) copy-start(bf16[1,1,4,256,96]{3,4,2,1,0:T(8,128)(2,1)} %param.5) | copy-start | bytes 589828
  7.2 15.4 %copy-start.4 = (bf16[1,1,4,256,96]{3,4,2,1,0:T(8,128)(2,1)S(1)}, bf16[1,1,4,256,96]{3,4,2,1,0:T(8,128)(2,1)}, u32[]{:S(2)}) copy-start(bf16[1,1,4,256,96]{3,4,2,1,0:T(8,128)(2,1)} %param.4) | copy-start | bytes 589828
  7.2 214.5 %all-reduce.8.cloned.1.call-start = ((), (), s32[]{:S(2)}) async-start(), calls=%async_computation | async-start | bytes 2654208 | tf_op jit(solution)/shard_map/psum | solution.py:96
  8.2 84.3 %collective-permute-start.1 = (bf16[1,1,256,96]{2,3,1,0:T(8,128)(2,1)S(1)}, bf16[1,1,256,96]{2,3,1,0:T(8,128)(2,1)S(1)}, u32[]{:S(2)}, u32[]{:S(2)}) collective-permute-start(bf16[1,1,256,96]{2,3,1,0:T(8,128)(2,1)S(1)} %get-tuple-element.73), channel_id=1, source_target_pairs={{2,0},{3,1},{6,4},{7,5},{10,8},{11,9},{14,12},{15,13},{18,16},{19,... | collective-permute-start | bytes 147464 | tf_op jit(solution)/shard_map/ppermute | solution.py:15
  9.4 83.1 %collective-permute-start = (bf16[1,1,256,96]{2,3,1,0:T(8,128)(2,1)S(1)}, bf16[1,1,256,96]{2,3,1,0:T(8,128)(2,1)S(1)}, u32[]{:S(2)}, u32[]{:S(2)}) collective-permute-start(bf16[1,1,256,96]{2,3,1,0:T(8,128)(2,1)S(1)} %get-tuple-element.72), channel_id=1, source_target_pairs={{0,2},{1,3},{4,6},{5,7},{8,10},{9,11},{12,14},{13,15},{16,18},{17,... | collective-permute-start | bytes 147464 | tf_op jit(solution)/shard_map/ppermute | solution.py:14
  15.4 80.2 %collective-permute-start.5 = (bf16[1,1,256,96]{2,3,1,0:T(8,128)(2,1)S(1)}, bf16[1,1,256,96]{2,3,1,0:T(8,128)(2,1)S(1)}, u32[]{:S(2)}, u32[]{:S(2)}) collective-permute-start(bf16[1,1,256,96]{2,3,1,0:T(8,128)(2,1)S(1)} %get-tuple-element.69), channel_id=1, source_target_pairs={{2,0},{3,1},{6,4},{7,5},{10,8},{11,9},{14,12},{15,13},{18,16},{19,... | collective-permute-start | bytes 147464 | tf_op jit(solution)/shard_map/ppermute | solution.py:15
  16.7 78.9 %collective-permute-start.4 = (bf16[1,1,256,96]{2,3,1,0:T(8,128)(2,1)S(1)}, bf16[1,1,256,96]{2,3,1,0:T(8,128)(2,1)S(1)}, u32[]{:S(2)}, u32[]{:S(2)}) collective-permute-start(bf16[1,1,256,96]{2,3,1,0:T(8,128)(2,1)S(1)} %get-tuple-element.68), channel_id=1, source_target_pairs={{0,2},{1,3},{4,6},{5,7},{8,10},{9,11},{12,14},{13,15},{16,18},{17,... | collective-permute-start | bytes 147464 | tf_op jit(solution)/shard_map/ppermute | solution.py:14
  22.3 1.1 copy-start.5
  23.4 0.8 copy-start.18
  92.5 19.2 %collective-permute-start.2 = (bf16[1,6,256,96]{2,3,1,0:T(8,128)(2,1)S(1)}, bf16[1,6,256,96]{2,3,1,0:T(8,128)(2,1)S(1)}, u32[]{:S(2)}, u32[]{:S(2)}) collective-permute-start(bf16[1,6,256,96]{2,3,1,0:T(8,128)(2,1)S(1)} %pad_maximum_fusion.17), channel_id=1, source_target_pairs={{8,0},{12,4},{9,1},{13,5},{10,2},{14,6},{11,3},{15,7},{24,16},{28,... | collective-permute-start | bytes 884744 | tf_op jit(solution)/shard_map/ppermute | solution.py:23
  93.8 18.4 %collective-permute-start.3 = (bf16[1,6,256,96]{2,3,1,0:T(8,128)(2,1)S(1)}, bf16[1,6,256,96]{2,3,1,0:T(8,128)(2,1)S(1)}, u32[]{:S(2)}, u32[]{:S(2)}) collective-permute-start(bf16[1,6,256,96]{2,3,1,0:T(8,128)(2,1)S(1)} %pad_maximum_fusion.17), channel_id=1, source_target_pairs={{4,0},{8,4},{12,8},{5,1},{9,5},{13,9},{6,2},{10,6},{14,10},{7,3},{... | collective-permute-start | bytes 884744 | tf_op jit(solution)/shard_map/ppermute | solution.py:23
  95.6 17.3 %collective-permute-start.6 = (bf16[1,6,256,96]{2,3,1,0:T(8,128)(2,1)S(1)}, bf16[1,6,256,96]{2,3,1,0:T(8,128)(2,1)S(1)}, u32[]{:S(2)}, u32[]{:S(2)}) collective-permute-start(bf16[1,6,256,96]{2,3,1,0:T(8,128)(2,1)S(1)} %pad_maximum_fusion.18), channel_id=1, source_target_pairs={{0,8},{4,12},{1,9},{5,13},{2,10},{6,14},{3,11},{7,15},{16,24},{20,... | collective-permute-start | bytes 884744 | tf_op jit(solution)/shard_map/ppermute | solution.py:23
  101.7 18.6 %collective-permute-start.7 = (bf16[1,6,256,96]{2,3,1,0:T(8,128)(2,1)S(1)}, bf16[1,6,256,96]{2,3,1,0:T(8,128)(2,1)S(1)}, u32[]{:S(2)}, u32[]{:S(2)}) collective-permute-start(bf16[1,6,256,96]{2,3,1,0:T(8,128)(2,1)S(1)} %pad_maximum_fusion.18), channel_id=1, source_target_pairs={{0,4},{4,8},{8,12},{1,5},{5,9},{9,13},{2,6},{6,10},{10,14},{3,7},{... | collective-permute-start | bytes 884744 | tf_op jit(solution)/shard_map/ppermute | solution.py:23
  125.8 1.1 copy-start.3
  126.8 1.3 copy-start.12
  126.8 1.6 copy-start.11
  128.1 0.9 copy-start.10
  128.4 1.1 copy-start.1
  128.4 1.1 copy-start.9
  129.0 1.1 copy-start.2
  129.0 1.1 copy-start.8
  129.5 0.9 copy-start.7
  130.1 0.9 copy-start.13
  130.1 1.0 copy-start.14
  130.1 1.1 copy-start.15
  130.1 1.2 copy-start.17
  130.8 1.1 copy-start.6
  130.8 1.1 copy-start.16
Sparse Core Ops, SparseCore 0:
  127.0 94.7 all-reduce.7
where the time goes:
time: 232 us; the launch traced here: 231 us
  waiting for transfers between devices  88.7 us (38%)
  blocking collectives  59.7 us (26%)
  local copies, waits for them, and re-layouts  30.5 us (13%)
  starting transfers between devices  24.8 us (11%)
  between operations  14.9 us (6%)
  matrix products  7.44 us (3%)
  other arithmetic  5.05 us (2%)
    psum x1, waiting for transfers between devices, on_device(): kernel_total = lax.psum(kernel_local, ('tm', 'space', 'dp'))  88.6 us
    psum x1, blocking collectives, on_device(): sketch_total = lax.psum(sketch_terms, ('tm', 'space', 'dp'))  59.7 us
    unnamed x71, local copies, waits for them, and re-layouts  17.4 us
    ppermute x4, starting transfers between devices, passed_along(): return lax.ppermute(block, axis, route)  12.8 us
    ppermute x2, starting transfers between devices, padded(): before = lax.ppermute(last, axis, up)  9.42 us
  transfers between devices with their start and end apart: 9, of which 1 were waited for; matrix products, arithmetic and copies ran while one was open for 13% of the time, Pallas kernels for 0%

commit v1 on v0

--- a/solution.py
+++ b/solution.py
@@ -92,7 +92,8 @@
         * lax.axis_size("space")
         * lax.axis_size("dp")
     )
-    sketch_total = lax.psum(sketch_terms, ("tm", "space", "dp"))
+    parts = lax.all_gather(sketch_terms, ("tm", "space", "dp"), axis=0, tiled=False)
+    sketch_total = parts.sum(axis=0)
     kernel_total = lax.psum(kernel_local, ("tm", "space", "dp"))
     sketches = sketch_total / jnp.float32(total_pixels)
     weight_grad = kernel_total * (1.0 / jnp.sqrt(jnp.float32(total_pixels)))

time: 232 us -> 196 us (0.84)
  blocking collectives: 59.7 us -> 22.1 us
    psum x1 -> x0, blocking collectives: 59.7 us -> none  [on_device(): sketch_total = lax.psum(sketch_terms, ('tm', 'space', 'dp'))]
    all_gather x0 -> x1, blocking collectives: none -> 22.1 us  [on_device(): lax.all_gather(sketch_terms, ('tm', 'space', 'dp'), axis=0, tiled=False)]
  transfers between devices with their start and end apart: 9 -> 9, of which waited for: 1 -> 1; matrix products, arithmetic and copies ran while one was open for 13% -> 16% of each run, Pallas kernels for 0% -> 0%
where the time goes in v1:
time: 196 us
  waiting for transfers between devices  91 us (46%)
  local copies, waits for them, and re-layouts  30.5 us (16%)
  starting transfers between devices  24.8 us (13%)
  blocking collectives  22.1 us (11%)
  between operations  14.9 us (8%)
  matrix products  7.42 us (4%)
  other arithmetic  5.12 us (3%)
    psum x1, waiting for transfers between devices, on_device(): kernel_total = lax.psum(kernel_local, ('tm', 'space', 'dp'))  90.9 us
    all_gather x1, blocking collectives, on_device(): lax.all_gather(sketch_terms, ('tm', 'space', 'dp'), axis=0, tiled=False)  22.1 us
    unnamed x71, local copies, waits for them, and re-layouts  17.4 us
    ppermute x4, starting transfers between devices, passed_along(): return lax.ppermute(block, axis, route)  12.8 us
    ppermute x2, starting transfers between devices, padded(): before = lax.ppermute(last, axis, up)  9.42 us
  transfers between devices with their start and end apart: 9, of which 1 were waited for; matrix products, arithmetic and copies ran while one was open for 16% of the time, Pallas kernels for 0%

profile of v1, /device:TPU:0, one launch (start us, length us, event | category | flops | bytes accessed | tf_op | source)
XLA Modules:
  0.0 195.8 jit_solution(17880652456468030082)
XLA Ops:
  7.2 0.9 fusion.34
  8.2 1.3 collective-permute-start.1
  9.4 4.9 %collective-permute-start = (bf16[1,1,256,96]{2,3,1,0:T(8,128)(2,1)S(1)}, bf16[1,1,256,96]{2,3,1,0:T(8,128)(2,1)S(1)}, u32[]{:S(2)}, u32[]{:S(2)}) collective-permute-start(bf16[1,1,256,96]{2,3,1,0:T(8,128)(2,1)S(1)} %get-tuple-element.75), channel_id=1, source_target_pairs={{0,2},{1,3},{4,6},{5,7},{8,10},{9,11},{12,14},{13,15},{16,18},{17,... | collective-permute-start | bytes 147464 | tf_op jit(solution)/shard_map/ppermute | solution.py:14
  14.3 1.0 fusion.27
  15.4 1.3 collective-permute-start.5
  16.7 4.5 %collective-permute-start.4 = (bf16[1,1,256,96]{2,3,1,0:T(8,128)(2,1)S(1)}, bf16[1,1,256,96]{2,3,1,0:T(8,128)(2,1)S(1)}, u32[]{:S(2)}, u32[]{:S(2)}) collective-permute-start(bf16[1,1,256,96]{2,3,1,0:T(8,128)(2,1)S(1)} %get-tuple-element.71), channel_id=1, source_target_pairs={{0,2},{1,3},{4,6},{5,7},{8,10},{9,11},{12,14},{13,15},{16,18},{17,... | collective-permute-start | bytes 147464 | tf_op jit(solution)/shard_map/ppermute | solution.py:14
  21.2 1.1 copy.63
  22.9 0.6 copy-done.5
  23.7 0.5 copy-done.18
  24.6 22.1 %all-gather = f32[32,96,32]{1,2,0:T(8,128)S(1)} all-gather(f32[2,96,32]{1,2,0:T(8,128)S(1)} %pad_maximum_fusion.19), channel_id=2, replica_groups=mesh['groups'=2,'tm'=4,'space'=2,'dp'=2] {'tm','space','dp'}, dimensions={0}, use_global_device_ids=true | all-gather | bytes 417792 | tf_op jit(solution)/shard_map/all_gather | solution.py:95
  46.8 0.6 broadcast_multiply_fusion.1
  47.5 0.7 copy.75
  48.3 0.7 copy.76
  49.0 0.7 copy.77
  49.8 0.7 copy.78
  50.5 0.7 copy.79
  51.2 0.7 copy.80
  52.0 0.7 copy.81
  52.7 0.7 copy.82
  53.5 0.7 copy.92
  54.2 0.7 copy.83
  55.0 1.3 collective-permute-start.2
  56.3 1.3 collective-permute-start.3
  58.1 6.1 %collective-permute-start.6 = (bf16[1,6,256,96]{2,3,1,0:T(8,128)(2,1)S(1)}, bf16[1,6,256,96]{2,3,1,0:T(8,128)(2,1)S(1)}, u32[]{:S(2)}, u32[]{:S(2)}) collective-permute-start(bf16[1,6,256,96]{2,3,1,0:T(8,128)(2,1)S(1)} %pad_maximum_fusion.18), channel_id=1, source_target_pairs={{0,8},{4,12},{1,9},{5,13},{2,10},{6,14},{3,11},{7,15},{16,24},{20,... | collective-permute-start | bytes 884744 | tf_op jit(solution)/shard_map/ppermute | solution.py:23
  64.2 4.1 %collective-permute-start.7 = (bf16[1,6,256,96]{2,3,1,0:T(8,128)(2,1)S(1)}, bf16[1,6,256,96]{2,3,1,0:T(8,128)(2,1)S(1)}, u32[]{:S(2)}, u32[]{:S(2)}) collective-permute-start(bf16[1,6,256,96]{2,3,1,0:T(8,128)(2,1)S(1)} %pad_maximum_fusion.18), channel_id=1, source_target_pairs={{0,4},{4,8},{8,12},{1,5},{5,9},{9,13},{2,6},{6,10},{10,14},{3,7},{... | collective-permute-start | bytes 884744 | tf_op jit(solution)/shard_map/ppermute | solution.py:23
  69.4 0.5 copy.55
  70.1 0.7 copy.93
  71.0 0.7 copy.91
  72.2 0.9 copy.94
  73.6 0.5 copy.73
  75.9 0.5 copy.43
  76.4 0.5 copy.45
  77.0 0.5 copy.47
  77.6 0.5 copy.49
  78.2 0.5 copy.51
  78.6 0.9 copy.88
  80.0 0.9 copy.89
  81.0 0.5 copy.64
  81.6 0.5 copy.65
  82.2 0.5 copy.66
  83.3 0.5 copy.67
  83.9 0.7 copy.68
  84.8 0.5 copy.69
  88.2 1.1 copy-done.3
  89.3 1.2 fusion.35
  94.8 0.7 copy.74
  95.5 90.9 %all-reduce.8.cloned.1.call-done = f32[3,3,3,96,96]{4,3,2,1,0:T(8,128)} async-done(((f32[3,3,3,96,96]{4,3,2,1,0:T(8,128)}), f32[3,3,3,96,96]{4,3,2,1,0:T(8,128)}) %all-reduce.8.cloned.1.call-update) | async-done | bytes 995344 | tf_op jit(solution)/shard_map/psum | solution.py:97
  186.5 2.5 %broadcast_multiply_fusion = f32[3,3,3,96,96]{4,3,2,1,0:T(8,128)} fusion(f32[3,3,3,96,96]{4,3,2,1,0:T(8,128)} %all-reduce.8.cloned.1.call-done), kind=kLoop, calls=%fused_computation.32 | loop fusion | flops 248832 | bytes 1990656 | tf_op jit(solution)/shard_map/mul | solution.py:99
  (117 shorter events, 15.2 us)
Async XLA Ops:
  7.2 15.2 %copy-start = (bf16[1,1,4,256,96]{3,4,2,1,0:T(8,128)(2,1)S(1)}, bf16[1,1,4,256,96]{3,4,2,1,0:T(8,128)(2,1)}, u32[]{:S(2)}) copy-start(bf16[1,1,4,256,96]{3,4,2,1,0:T(8,128)(2,1)} %param.5) | copy-start | bytes 589828
  7.2 15.4 %copy-start.4 = (bf16[1,1,4,256,96]{3,4,2,1,0:T(8,128)(2,1)S(1)}, bf16[1,1,4,256,96]{3,4,2,1,0:T(8,128)(2,1)}, u32[]{:S(2)}) copy-start(bf16[1,1,4,256,96]{3,4,2,1,0:T(8,128)(2,1)} %param.4) | copy-start | bytes 589828
  7.2 179.3 %all-reduce.8.cloned.1.call-start = ((), (), s32[]{:S(2)}) async-start(), calls=%async_computation | async-start | bytes 2654208 | tf_op jit(solution)/shard_map/psum | solution.py:97
  8.2 46.8 %collective-permute-start.1 = (bf16[1,1,256,96]{2,3,1,0:T(8,128)(2,1)S(1)}, bf16[1,1,256,96]{2,3,1,0:T(8,128)(2,1)S(1)}, u32[]{:S(2)}, u32[]{:S(2)}) collective-permute-start(bf16[1,1,256,96]{2,3,1,0:T(8,128)(2,1)S(1)} %get-tuple-element.76), channel_id=1, source_target_pairs={{2,0},{3,1},{6,4},{7,5},{10,8},{11,9},{14,12},{15,13},{18,16},{19,... | collective-permute-start | bytes 147464 | tf_op jit(solution)/shard_map/ppermute | solution.py:15
  9.4 45.5 %collective-permute-start = (bf16[1,1,256,96]{2,3,1,0:T(8,128)(2,1)S(1)}, bf16[1,1,256,96]{2,3,1,0:T(8,128)(2,1)S(1)}, u32[]{:S(2)}, u32[]{:S(2)}) collective-permute-start(bf16[1,1,256,96]{2,3,1,0:T(8,128)(2,1)S(1)} %get-tuple-element.75), channel_id=1, source_target_pairs={{0,2},{1,3},{4,6},{5,7},{8,10},{9,11},{12,14},{13,15},{16,18},{17,... | collective-permute-start | bytes 147464 | tf_op jit(solution)/shard_map/ppermute | solution.py:14
  15.4 42.6 %collective-permute-start.5 = (bf16[1,1,256,96]{2,3,1,0:T(8,128)(2,1)S(1)}, bf16[1,1,256,96]{2,3,1,0:T(8,128)(2,1)S(1)}, u32[]{:S(2)}, u32[]{:S(2)}) collective-permute-start(bf16[1,1,256,96]{2,3,1,0:T(8,128)(2,1)S(1)} %get-tuple-element.72), channel_id=1, source_target_pairs={{2,0},{3,1},{6,4},{7,5},{10,8},{11,9},{14,12},{15,13},{18,16},{19,... | collective-permute-start | bytes 147464 | tf_op jit(solution)/shard_map/ppermute | solution.py:15
  16.7 41.3 %collective-permute-start.4 = (bf16[1,1,256,96]{2,3,1,0:T(8,128)(2,1)S(1)}, bf16[1,1,256,96]{2,3,1,0:T(8,128)(2,1)S(1)}, u32[]{:S(2)}, u32[]{:S(2)}) collective-permute-start(bf16[1,1,256,96]{2,3,1,0:T(8,128)(2,1)S(1)} %get-tuple-element.71), channel_id=1, source_target_pairs={{0,2},{1,3},{4,6},{5,7},{8,10},{9,11},{12,14},{13,15},{16,18},{17,... | collective-permute-start | bytes 147464 | tf_op jit(solution)/shard_map/ppermute | solution.py:14
  22.3 1.1 copy-start.5
  23.4 0.8 copy-start.18
  55.0 19.2 %collective-permute-start.2 = (bf16[1,6,256,96]{2,3,1,0:T(8,128)(2,1)S(1)}, bf16[1,6,256,96]{2,3,1,0:T(8,128)(2,1)S(1)}, u32[]{:S(2)}, u32[]{:S(2)}) collective-permute-start(bf16[1,6,256,96]{2,3,1,0:T(8,128)(2,1)S(1)} %pad_maximum_fusion.17), channel_id=1, source_target_pairs={{8,0},{12,4},{9,1},{13,5},{10,2},{14,6},{11,3},{15,7},{24,16},{28,... | collective-permute-start | bytes 884744 | tf_op jit(solution)/shard_map/ppermute | solution.py:23
  56.3 18.4 %collective-permute-start.3 = (bf16[1,6,256,96]{2,3,1,0:T(8,128)(2,1)S(1)}, bf16[1,6,256,96]{2,3,1,0:T(8,128)(2,1)S(1)}, u32[]{:S(2)}, u32[]{:S(2)}) collective-permute-start(bf16[1,6,256,96]{2,3,1,0:T(8,128)(2,1)S(1)} %pad_maximum_fusion.17), channel_id=1, source_target_pairs={{4,0},{8,4},{12,8},{5,1},{9,5},{13,9},{6,2},{10,6},{14,10},{7,3},{... | collective-permute-start | bytes 884744 | tf_op jit(solution)/shard_map/ppermute | solution.py:23
  58.1 17.3 %collective-permute-start.6 = (bf16[1,6,256,96]{2,3,1,0:T(8,128)(2,1)S(1)}, bf16[1,6,256,96]{2,3,1,0:T(8,128)(2,1)S(1)}, u32[]{:S(2)}, u32[]{:S(2)}) collective-permute-start(bf16[1,6,256,96]{2,3,1,0:T(8,128)(2,1)S(1)} %pad_maximum_fusion.18), channel_id=1, source_target_pairs={{0,8},{4,12},{1,9},{5,13},{2,10},{6,14},{3,11},{7,15},{16,24},{20,... | collective-permute-start | bytes 884744 | tf_op jit(solution)/shard_map/ppermute | solution.py:23
  64.2 18.6 %collective-permute-start.7 = (bf16[1,6,256,96]{2,3,1,0:T(8,128)(2,1)S(1)}, bf16[1,6,256,96]{2,3,1,0:T(8,128)(2,1)S(1)}, u32[]{:S(2)}, u32[]{:S(2)}) collective-permute-start(bf16[1,6,256,96]{2,3,1,0:T(8,128)(2,1)S(1)} %pad_maximum_fusion.18), channel_id=1, source_target_pairs={{0,4},{4,8},{8,12},{1,5},{5,9},{9,13},{2,6},{6,10},{10,14},{3,7},{... | collective-permute-start | bytes 884744 | tf_op jit(solution)/shard_map/ppermute | solution.py:23
  88.2 1.1 copy-start.3
  89.3 1.3 copy-start.12
  89.3 1.6 copy-start.11
  90.5 0.9 copy-start.10
  90.9 1.1 copy-start.1
  90.9 1.1 copy-start.9
  91.4 1.1 copy-start.2
  91.4 1.1 copy-start.8
  91.9 0.9 copy-start.7
  92.5 0.9 copy-start.13
  92.5 1.0 copy-start.14
  92.5 1.1 copy-start.15
  92.5 1.2 copy-start.17
  93.2 1.1 copy-start.6
  93.2 1.1 copy-start.16
Sparse Core Ops, SparseCore 0:
  89.4 97.0 all-reduce.7
